TPU v7x, 32 devices: a whole 2x2x4 slice. The times are simulated.
32 devices in a mesh: dp: 8 (over z, core), rot: 4 (over y, x).
Axes of the slice: x: 2, y: 2, z: 4, core: 2. Of those that a mesh axis runs over, the one named last changes fastest.
Arguments:
- vectors: bfloat16 [2048, 4096], P('dp', 'rot'), may hold values from -100 to 100
- rotation: bfloat16 [4096, 4096], P('rot'), may hold values from -0.125 to 0.125
- codes: int32 [2048, 256], P('dp', 'rot'), may hold values from 0 to 255
Outputs:
- codebook: float32 [4096, 256], P('rot')
- new_rotation: bfloat16 [4096, 4096], P('rot', 'dp')
All inputs are finite; a program needn't handle non-finite values.
Results may differ from a plain program's by a relative error of at most 0.007.
Values may be sent and summed in bfloat16 or wider, within the bound.
No kernel may reach another device: no remote copies, remote signals or barrier semaphores. Data moves between devices by JAX's collectives and lax.ppermute only.
A program may use at most 64 MiB of HBM per device.

v0:
```python
import math
import jax
import jax.numpy as jnp
from jax import lax
from jax.sharding import PartitionSpec as P

K = 256
ITERS = 2


def body(vectors, rotation, codes):
    row_count, block_dims = vectors.shape
    width = rotation.shape[1]
    local_spaces = codes.shape[1]
    sub_dims = block_dims // local_spaces
    tile_cols = width // lax.axis_size("dp")
    tile_spaces = tile_cols // sub_dims
    dp_index = lax.axis_index("dp")
    code_ids = jnp.arange(K, dtype=jnp.int32)
    dp_size = lax.axis_size("dp")
    row_codes = lax.all_gather(codes, "rot", axis=1, tiled=True)

    def block_codes(block):
        return lax.dynamic_slice_in_dim(row_codes, block * tile_spaces, tile_spaces, 1).astype(
            jnp.bfloat16
        )

    if dp_size % 2:
        parts = [jnp.concatenate([vectors, block_codes(dp_index)], axis=1)]
        for shift in range(1, dp_size):
            pairs = [(i, (i + shift) % dp_size) for i in range(dp_size)]
            target = (dp_index + shift) % dp_size
            parts.append(
                lax.ppermute(jnp.concatenate([vectors, block_codes(target)], axis=1), "dp", pairs)
            )
        joined = jnp.concatenate(parts, axis=0)
    else:

        def pair_part(block):
            return jnp.concatenate([vectors, block_codes(block), block_codes(block ^ 1)], axis=1)

        parts = [pair_part(dp_index)]
        for shift in range(2, dp_size, 2):
            pairs = [(i, (i + shift) % dp_size) for i in range(dp_size)]
            parts.append(lax.ppermute(pair_part((dp_index + shift) % dp_size), "dp", pairs))
        group = jnp.concatenate(parts, axis=0)
        mine = group[:, : block_dims + tile_spaces]
        for_mate = jnp.concatenate(
            [group[:, :block_dims], group[:, block_dims + tile_spaces :]], axis=1
        )
        mates = [(i, i ^ 1) for i in range(dp_size)]
        joined = jnp.concatenate([mine, lax.ppermute(for_mate, "dp", mates)], axis=0)
    all_vectors = joined[:, :block_dims]
    tile_codes = joined[:, block_dims:].astype(jnp.int32)
    rotated_t = lax.psum_scatter(
        lax.dot_general(
            rotation, vectors, (((0,), (1,)), ((), ())), preferred_element_type=jnp.float32
        ),
        "rot",
        scatter_dimension=0,
        tiled=True,
    ).astype(jnp.bfloat16)
    code_indicator = (codes.T[:, :, None] == code_ids[None, None, :]).astype(jnp.bfloat16)
    grouped_vectors = rotated_t.reshape(local_spaces, sub_dims, row_count)
    shard_code_sums = jnp.einsum(
        "vzo,voc->vzc", grouped_vectors, code_indicator, preferred_element_type=jnp.float32
    )
    local_counts = jnp.sum(code_indicator, axis=1, dtype=jnp.float32)
    total_sums, total_counts = lax.psum((shard_code_sums, local_counts), "dp")
    book = total_sums / jnp.maximum(total_counts, 1.0)[:, None, :]
    codebook = book.reshape(block_dims, K)
    blocks_per_rot = local_spaces // tile_spaces
    offered = lax.dynamic_slice_in_dim(
        book.astype(jnp.bfloat16), dp_index % blocks_per_rot * tile_spaces, tile_spaces, 0
    )
    tile_book = lax.all_gather(offered, "rot", axis=0)[dp_index // blocks_per_rot]
    tile_book, all_vectors, tile_codes = lax.optimization_barrier(
        (tile_book, all_vectors, tile_codes)
    )
    rebuilt_t = jnp.take_along_axis(tile_book, tile_codes.T[:, None, :], axis=2)
    rebuilt_t = rebuilt_t.astype(jnp.bfloat16).reshape(tile_cols, all_vectors.shape[0])
    cross_tile = lax.dot_general(
        all_vectors, rebuilt_t, (((0,), (1,)), ((), ())), preferred_element_type=jnp.float32
    ).astype(jnp.bfloat16)

    def apply_gram(rows_b, gram_b):
        return jnp.dot(
            rows_b,
            lax.all_gather(gram_b, "rot", axis=0, tiled=True),
            preferred_element_type=jnp.float32,
        )

    columns = cross_tile
    new_tile = None
    for iteration in range(ITERS):
        rows_b = lax.all_gather(columns, "dp", axis=1, tiled=True)
        partial = lax.dot_general(
            rows_b, columns, (((0,), (0,)), ((), ())), preferred_element_type=jnp.float32
        ).astype(jnp.bfloat16)
        if iteration == 0:
            gram_part = lax.psum_scatter(partial, "rot", scatter_dimension=0, tiled=True)
        else:
            gram_part = lax.psum(partial, "rot")
        if iteration == 0:
            gram_f = gram_part.astype(jnp.float32)
            total = lax.psum(jnp.sum(gram_f * gram_f), ("dp", "rot"))
            factor = 1.7 / jnp.sqrt(jnp.sqrt(total))
            product = apply_gram(rows_b, gram_part)
            new_tile = factor * (
                1.5 * columns.astype(jnp.float32) - 0.5 * (factor * factor) * product
            )
        else:
            product = jnp.dot(rows_b, gram_part, preferred_element_type=jnp.float32)
            new_tile = 1.5 * columns.astype(jnp.float32) - 0.5 * product
        columns = new_tile.astype(jnp.bfloat16)
    new_rotation = (math.sqrt(width) * new_tile).astype(jnp.bfloat16)
    return (codebook, new_rotation)


def solution(mesh):
    return jax.shard_map(
        body,
        mesh=mesh,
        in_specs=(P("dp", "rot"), P("rot", None), P("dp", "rot")),
        out_specs=(P("rot", None), P("rot", "dp")),
        check_vma=False,
    )
```

profile of v0, /device:TPU:0, one launch (start us, length us, event | category | flops | bytes accessed | tf_op | source)
XLA Modules:
  0.0 1250.6 jit_solution(5058009144251274857)
XLA Ops:
  7.2 7.8 fusion.17
  16.4 11.0 all_gather.20
  29.3 3.0 collective-permute-start.1
  33.4 3.4 convert_reduce_fusion
  36.9 8.4 collective-permute-done
  45.3 19.9 %collective-permute-done.1 = bf16[256,1088]{0,1:T(8,128)(2,1)S(1)} collective-permute-done((bf16[256,1088]{0,1:T(8,128)(2,1)S(1)}, bf16[256,1088]{0,1:T(8,128)(2,1)S(1)}, u32[]{:S(2)}, u32[]{:S(2)}) %collective-permute-start.1) | collective-permute-done | bytes 557088 | tf_op jit(solution)/shard_map/ppermute | solution.py:45
  72.5 5.1 fusion.1
  77.7 4.2 fusion.14
  81.9 64.6 %all-reduce.6.cloned.1.call-done = (f32[64,16,256]{2,1,0:T(8,128)}, f32[64,256]{1,0:T(8,128)}) async-done(((f32[64,16,256]{2,1,0:T(8,128)}, f32[64,256]{1,0:T(8,128)}), (f32[64,16,256]{2,1,0:T(8,128)}, f32[64,256]{1,0:T(8,128)})) %all-reduce.6.cloned.1.call-update) | async-done | bytes 1114128 | tf_op jit(solution)/shard_map/psum | solution.py:69
  150.7 3.4 fusion.8
  154.1 21.1 %all-gather.12.cloned.1.call-done = bf16[128,16,256]{2,1,0:T(8,128)(2,1)} async-done(((bf16[32,16,256]{2,1,0:T(8,128)(2,1)}), bf16[128,16,256]{2,1,0:T(8,128)(2,1)}) %all-gather.12.cloned.1.call-update) | async-done | bytes 1048592 | tf_op jit(solution)/shard_map/all_gather | solution.py:76
  177.4 634.4 %gather_fusion = bf16[65536,16]{1,0:T(8,128)(2,1)} fusion(bf16[32,16,256]{1,2,0:T(8,128)(2,1)S(1)} %bitcast.37, s32[65536]{0:T(1024)S(1)} %bitcast.36), kind=kCustom, calls=%fused_computation | custom fusion | bytes 4718592 | tf_op jit(solution)/shard_map/jit(take_along_axis)/gather | solution.py:80
  811.8 12.8 %copy.32 = bf16[32,2048,16]{1,2,0:T(8,128)(2,1)S(1)} copy(bf16[32,2048,16]{2,1,0:T(8,128)(2,1)} %bitcast.38) | data formatting | bytes 4194304 | tf_op jit(solution)/shard_map/jit(take_along_axis)/gather | solution.py:80
  826.8 3.3 convolution_convert_fusion.2
  830.4 82.0 %all-gather.6.cloned.1.call-done = bf16[1024,4096]{1,0:T(8,128)(2,1)} async-done(((bf16[1024,512]{1,0:T(8,128)(2,1)}), bf16[1024,4096]{1,0:T(8,128)(2,1)}) %all-gather.6.cloned.1.call-update) | async-done | bytes 8388624 | tf_op jit(solution)/shard_map/all_gather | solution.py:96
  912.4 10.2 convolution_convert_fusion.1
  922.6 51.2 %reduce-scatter.5.cloned.1.call-done = bf16[1024,512]{1,0:T(8,128)(2,1)} async-done(((bf16[4096,512]{1,0:T(8,128)(2,1)}), bf16[1024,512]{1,0:T(8,128)(2,1)}) %reduce-scatter.5.cloned.1.call-update) | async-done | bytes 1048592 | tf_op jit(solution)/shard_map/reduce_scatter | solution.py:101
  976.3 40.4 %psum.30 = f32[]{:T(128)} all-reduce(f32[]{:T(128)} %multiply_reduce_fusion), channel_id=1, replica_groups=mesh['dp'=8,'rot'=4] {'dp','rot'}, use_global_device_ids=true, to_apply=%region_6.7 | all-reduce | flops 1 | bytes 8 | tf_op jit(solution)/shard_map/psum | solution.py:106
  1017.3 11.5 all-gather.8.cloned.1.call-done
  1028.9 10.1 multiply_convert_fusion.1
  1039.3 81.9 %all-gather.10.cloned.1.call-done = bf16[1024,4096]{1,0:T(8,128)(2,1)} async-done(((bf16[1024,512]{1,0:T(8,128)(2,1)}), bf16[1024,4096]{1,0:T(8,128)(2,1)}) %all-gather.10.cloned.1.call-update) | async-done | bytes 8388624 | tf_op jit(solution)/shard_map/all_gather | solution.py:96
  1121.2 10.1 convolution_convert_fusion
  1131.3 102.3 %all-reduce.4.cloned.1.call-done = bf16[4096,512]{1,0:T(8,128)(2,1)} async-done(((bf16[4096,512]{1,0:T(8,128)(2,1)}), bf16[4096,512]{1,0:T(8,128)(2,1)}) %all-reduce.4.cloned.1.call-update) | async-done | bytes 4194320 | tf_op jit(solution)/shard_map/psum | solution.py:103
  1233.6 10.1 multiply_convert_fusion
  (56 shorter events, 23.1 us)
Async XLA Ops:
  7.2 64.0 %reduce-scatter.3.cloned.1.call-start = ((), (), s32[]{:S(2)}) async-start(), calls=%async_computation.2 | async-start | bytes 5242880 | tf_op jit(solution)/shard_map/reduce_scatter | solution.py:55
  15.1 1.0 copy-start.6
  15.1 1.3 copy-start.7
  15.1 131.4 %all-reduce.6.cloned.1.call-start = ((), (), s32[]{:S(2)}) async-start(), calls=%async_computation.9 | async-start | bytes 2228224 | tf_op jit(solution)/shard_map/psum | solution.py:69
  27.5 17.8 %collective-permute-start = (bf16[256,1088]{0,1:T(8,128)(2,1)S(1)}, bf16[256,1088]{0,1:T(8,128)(2,1)S(1)}, u32[]{:S(2)}, u32[]{:S(2)}) collective-permute-start(bf16[256,1088]{0,1:T(8,128)(2,1)S(1)} %get-tuple-element.10), channel_id=1, source_target_pairs={{0,8},{4,12},{8,16},{12,20},{16,24},{20,28},{24,0},{28,4},{1,9},{5... | collective-permute-start | bytes 1671176 | tf_op jit(solution)/shard_map/ppermute | solution.py:45
  29.3 35.9 %collective-permute-start.1 = (bf16[256,1088]{0,1:T(8,128)(2,1)S(1)}, bf16[256,1088]{0,1:T(8,128)(2,1)S(1)}, u32[]{:S(2)}, u32[]{:S(2)}) collective-permute-start(bf16[256,1088]{0,1:T(8,128)(2,1)S(1)} %get-tuple-element.11), channel_id=1, source_target_pairs={{0,16},{4,20},{8,24},{12,28},{16,0},{20,4},{24,8},{28,12},{1,17},{... | collective-permute-start | bytes 1671176 | tf_op jit(solution)/shard_map/ppermute | solution.py:45
  32.3 33.0 %collective-permute-start.2 = (bf16[256,1088]{0,1:T(8,128)(2,1)S(1)}, bf16[256,1088]{0,1:T(8,128)(2,1)S(1)}, u32[]{:S(2)}, u32[]{:S(2)}) collective-permute-start(bf16[256,1088]{0,1:T(8,128)(2,1)S(1)} %get-tuple-element.12), channel_id=1, source_target_pairs={{0,24},{4,28},{8,0},{12,4},{16,8},{20,12},{24,16},{28,20},{1,25},{... | collective-permute-start | bytes 1671176 | tf_op jit(solution)/shard_map/ppermute | solution.py:45
  65.2 0.8 copy-start.1
  65.2 1.0 copy-start.2
  77.6 97.6 %all-gather.12.cloned.1.call-start = ((), (), s32[]{:S(2)}) async-start(), calls=%async_computation.8 | async-start | bytes 1310720 | tf_op jit(solution)/shard_map/all_gather | solution.py:76
  81.9 67.9 %collective-permute-start.3 = (bf16[1024,1056]{0,1:T(8,128)(2,1)}, bf16[1024,1056]{0,1:T(8,128)(2,1)}, u32[]{:S(2)}, u32[]{:S(2)}) collective-permute-start(bf16[1024,1056]{0,1:T(8,128)(2,1)} %fusion.14), channel_id=1, source_target_pairs={{0,4},{4,0},{8,12},{12,8},{16,20},{20,16},{24,28},{28,24},{1,5},{5... | collective-permute-start | bytes 6488072 | tf_op jit(solution)/shard_map/ppermute | solution.py:52
  148.7 2.0 copy-start.3
  149.5 762.8 %all-gather.6.cloned.1.call-start = ((), (), s32[]{:S(2)}) async-start(), calls=%async_computation.3 | async-start | bytes 9437184 | tf_op jit(solution)/shard_map/all_gather | solution.py:96
  824.6 2.2 copy-start
  830.2 143.6 %reduce-scatter.5.cloned.1.call-start = ((), (), s32[]{:S(2)}) async-start(), calls=%async_computation.4 | async-start | bytes 5242880 | tf_op jit(solution)/shard_map/reduce_scatter | solution.py:101
  922.5 106.4 %copy-start.4 = (bf16[1024,512]{1,0:T(8,128)(2,1)S(1)}, bf16[1024,512]{1,0:T(8,128)(2,1)}, u32[]{:S(2)}) copy-start(bf16[1024,512]{1,0:T(8,128)(2,1)} %convolution_convert_fusion.2) | copy-start | bytes 3145732
  922.5 106.3 %all-gather.8.cloned.1.call-start = ((), (), s32[]{:S(2)}) async-start(), calls=%async_computation.5 | async-start | bytes 5242880 | tf_op jit(solution)/shard_map/all_gather | solution.py:89
  973.8 147.4 %all-gather.10.cloned.1.call-start = ((), (), s32[]{:S(2)}) async-start(), calls=%async_computation.6 | async-start | bytes 9437184 | tf_op jit(solution)/shard_map/all_gather | solution.py:96
  1039.0 194.6 %all-reduce.4.cloned.1.call-start = ((), (), s32[]{:S(2)}) async-start(), calls=%async_computation.7 | async-start | bytes 8388608 | tf_op jit(solution)/shard_map/psum | solution.py:103
  1131.3 102.3 %copy-start.5 = (bf16[1024,512]{1,0:T(8,128)(2,1)S(1)}, bf16[1024,512]{1,0:T(8,128)(2,1)}, u32[]{:S(2)}) copy-start(bf16[1024,512]{1,0:T(8,128)(2,1)} %multiply_convert_fusion.1) | copy-start | bytes 3145732
Sparse Core Ops, SparseCore 0:
  15.2 55.9 reduce-scatter.2
  77.7 68.7 all-reduce.5
  149.7 25.4 all-gather.11
  830.3 82.0 all-gather.5
  922.7 51.0 reduce-scatter.4
  975.5 53.3 all-gather.7
  1039.1 82.0 all-gather.9
  1131.5 102.0 all-reduce.3
where the time goes:
time: 1250 us
  local copies, waits for them, and re-layouts  656 us (52%)
  waiting for transfers between devices  444 us (36%)
  matrix products  56.8 us (5%)
  blocking collectives  51.4 us (4%)
  other arithmetic  20.8 us (2%)
  between operations  15.1 us (1%)
    gather x2, local copies, waits for them, and re-layouts, body(): rebuilt_t = jnp.take_along_axis(tile_book, tile_codes.T[:, None, :], axis=2)  647 us
    all_gather x2, waiting for transfers between devices, body(): rows_b = lax.all_gather(columns, 'dp', axis=1, tiled=True)  164 us
    psum x1, waiting for transfers between devices, body(): gram_part = lax.psum(partial, 'rot')  102 us
    psum x1, waiting for transfers between devices, body(): total_sums, total_counts = lax.psum((shard_code_sums, local_counts), 'dp')  64.6 us
    reduce_scatter x1, waiting for transfers between devices, body(): lax.psum_scatter(partial, 'rot', scatter_dimension=0, tiled=True)  51.2 us
    psum x1, blocking collectives, body(): total = lax.psum(jnp.sum(gram_f * gram_f), ('dp', 'rot'))  40.4 us
    ppermute x3, waiting for transfers between devices, body(): lax.ppermute(pair_part((dp_index + shift) % dp_size), 'dp', pairs)  28.4 us
  transfers between devices with their start and end apart: 12, of which 10 were waited for; matrix products, arithmetic and copies ran while one was open for 2% of the time, Pallas kernels for 0%

commit v1 on v0

--- a/solution.py
+++ b/solution.py
@@ -6,6 +6,18 @@
 
 K = 256
 ITERS = 2
+
+
+def gather_by_bits(x, axis, dim):
+    ways, here = (lax.axis_size(axis), lax.axis_index(axis))
+    grown, reach = (x, 1)
+    while reach < ways:
+        theirs = lax.ppermute(grown, axis, [(d, d ^ reach) for d in range(ways)])
+        mine_first = jnp.concatenate([grown, theirs], axis=dim)
+        theirs_first = jnp.concatenate([theirs, grown], axis=dim)
+        grown = jnp.where(here & reach == 0, mine_first, theirs_first)
+        reach = 2 * reach
+    return grown
 
 
 def body(vectors, rotation, codes):
@@ -93,7 +105,7 @@
     columns = cross_tile
     new_tile = None
     for iteration in range(ITERS):
-        rows_b = lax.all_gather(columns, "dp", axis=1, tiled=True)
+        rows_b = gather_by_bits(columns, "dp", 1)
         partial = lax.dot_general(
             rows_b, columns, (((0,), (0,)), ((), ())), preferred_element_type=jnp.float32
         ).astype(jnp.bfloat16)

time: 1250 us -> 1580 us (1.26)
  waiting for transfers between devices: 444 us -> 741 us
    ppermute x0 -> x6, waiting for transfers between devices: none -> 459 us  [gather_by_bits(): theirs = lax.ppermute(grown, axis, [(d, d ^ reach) for d in range(ways)])]
    all_gather x2 -> x0, waiting for transfers between devices: 164 us -> none  [body(): rows_b = lax.all_gather(columns, 'dp', axis=1, tiled=True)]
  transfers between devices with their start and end apart: 12 -> 16, of which waited for: 10 -> 14; matrix products, arithmetic and copies ran while one was open for 2% -> 1% of each run, Pallas kernels for 0% -> 0%
where the time goes in v1:
time: 1580 us
  waiting for transfers between devices  741 us (47%)
  local copies, waits for them, and re-layouts  662 us (42%)
  matrix products  60.3 us (4%)
  blocking collectives  51.6 us (3%)
  other arithmetic  31.6 us (2%)
    gather x2, local copies, waits for them, and re-layouts, body(): rebuilt_t = jnp.take_along_axis(tile_book, tile_codes.T[:, None, :], axis=2)  652 us
    ppermute x6, waiting for transfers between devices, gather_by_bits(): theirs = lax.ppermute(grown, axis, [(d, d ^ reach) for d in range(ways)])  459 us
    psum x1, waiting for transfers between devices, body(): gram_part = lax.psum(partial, 'rot')  104 us
    psum x1, waiting for transfers between devices, body(): total_sums, total_counts = lax.psum((shard_code_sums, local_counts), 'dp')  64.6 us
    reduce_scatter x1, waiting for transfers between devices, body(): lax.psum_scatter(partial, 'rot', scatter_dimension=0, tiled=True)  52.7 us
    psum x1, blocking collectives, body(): total = lax.psum(jnp.sum(gram_f * gram_f), ('dp', 'rot'))  40.5 us
  transfers between devices with their start and end apart: 16, of which 14 were waited for; matrix products, arithmetic and copies ran while one was open for 1% of the time, Pallas kernels for 0%

profile of v1, /device:TPU:0, one launch (start us, length us, event | category | flops | bytes accessed | tf_op | source)
XLA Modules:
  0.0 1576.4 jit_solution(1411329849431476164)
XLA Ops:
  7.2 7.9 fusion.21
  16.4 11.0 all_gather.14
  33.5 3.4 convert_reduce_fusion
  36.9 8.4 collective-permute-done
  45.3 19.9 %collective-permute-done.1 = bf16[256,1088]{0,1:T(8,128)(2,1)S(1)} collective-permute-done((bf16[256,1088]{0,1:T(8,128)(2,1)S(1)}, bf16[256,1088]{0,1:T(8,128)(2,1)S(1)}, u32[]{:S(2)}, u32[]{:S(2)}) %collective-permute-start.1) | collective-permute-done | bytes 557088 | tf_op jit(solution)/shard_map/ppermute | solution.py:57
  72.5 5.1 fusion.1
  77.7 4.2 fusion.14
  81.9 64.6 %all-reduce.6.cloned.1.call-done = (f32[64,16,256]{2,1,0:T(8,128)}, f32[64,256]{1,0:T(8,128)}) async-done(((f32[64,16,256]{2,1,0:T(8,128)}, f32[64,256]{1,0:T(8,128)}), (f32[64,16,256]{2,1,0:T(8,128)}, f32[64,256]{1,0:T(8,128)})) %all-reduce.6.cloned.1.call-update) | async-done | bytes 1114128 | tf_op jit(solution)/shard_map/psum | solution.py:81
  154.3 20.9 %all-gather.6.cloned.1.call-done = bf16[128,16,256]{2,1,0:T(8,128)(2,1)} async-done(((bf16[32,16,256]{2,1,0:T(8,128)(2,1)}), bf16[128,16,256]{2,1,0:T(8,128)(2,1)}) %all-gather.6.cloned.1.call-update) | async-done | bytes 1048592 | tf_op jit(solution)/shard_map/all_gather | solution.py:88
  177.5 639.2 %gather_fusion = bf16[65536,16]{1,0:T(8,128)(2,1)} fusion(bf16[32,16,256]{1,2,0:T(8,128)(2,1)S(1)} %bitcast.33, s32[65536]{0:T(1024)S(1)} %bitcast.32), kind=kCustom, calls=%fused_computation | custom fusion | bytes 4718592 | tf_op jit(solution)/shard_map/jit(take_along_axis)/gather | solution.py:92
  816.7 12.8 copy.36
  841.1 46.3 %collective-permute-done.5 = bf16[1024,1024]{0,1:T(8,128)(2,1)} collective-permute-done((bf16[1024,1024]{0,1:T(8,128)(2,1)S(1)}, bf16[1024,1024]{0,1:T(8,128)(2,1)}, u32[]{:S(2)}, u32[]{:S(2)}) %collective-permute-start.5) | collective-permute-done | bytes 2097184 | tf_op jit(solution)/shard_map/ppermute | solution.py:15
  887.4 4.9 maximum_select_fusion.2
  894.7 180.4 %collective-permute-done.6 = bf16[1024,2048]{0,1:T(8,128)(2,1)} collective-permute-done((bf16[1024,2048]{0,1:T(8,128)(2,1)}, bf16[1024,2048]{0,1:T(8,128)(2,1)}, u32[]{:S(2)}, u32[]{:S(2)}) %collective-permute-start.6) | collective-permute-done | bytes 4194336 | tf_op jit(solution)/shard_map/ppermute | solution.py:15
  1075.1 11.6 convolution_convert_fusion.1
  1086.7 52.7 %reduce-scatter.5.cloned.1.call-done = bf16[1024,512]{1,0:T(8,128)(2,1)} async-done(((bf16[4096,512]{1,0:T(8,128)(2,1)}), bf16[1024,512]{1,0:T(8,128)(2,1)}) %reduce-scatter.5.cloned.1.call-update) | async-done | bytes 1048592 | tf_op jit(solution)/shard_map/reduce_scatter | solution.py:113
  1141.8 40.5 %psum.30 = f32[]{:T(128)} all-reduce(f32[]{:T(128)} %multiply_reduce_fusion), channel_id=1, replica_groups=mesh['dp'=8,'rot'=4] {'dp','rot'}, use_global_device_ids=true, to_apply=%region_6.7 | all-reduce | flops 1 | bytes 8 | tf_op jit(solution)/shard_map/psum | solution.py:118
  1183.1 11.4 all-gather.4.cloned.1.call-done
  1194.5 9.8 multiply_convert_fusion.1
  1209.6 46.2 %collective-permute-done.8 = bf16[1024,1024]{0,1:T(8,128)(2,1)S(1)} collective-permute-done((bf16[1024,1024]{0,1:T(8,128)(2,1)S(1)}, bf16[1024,1024]{0,1:T(8,128)(2,1)S(1)}, u32[]{:S(2)}, u32[]{:S(2)}) %collective-permute-start.8) | collective-permute-done | bytes 2097184 | tf_op jit(solution)/shard_map/ppermute | solution.py:15
  1260.6 180.2 %collective-permute-done.9 = bf16[1024,2048]{0,1:T(8,128)(2,1)} collective-permute-done((bf16[1024,2048]{0,1:T(8,128)(2,1)S(1)}, bf16[1024,2048]{0,1:T(8,128)(2,1)}, u32[]{:S(2)}, u32[]{:S(2)}) %collective-permute-start.9) | collective-permute-done | bytes 4194336 | tf_op jit(solution)/shard_map/ppermute | solution.py:15
  1440.9 13.7 convolution_convert_fusion
  1454.6 103.7 %all-reduce.4.cloned.1.call-done = bf16[4096,512]{1,0:T(8,128)(2,1)} async-done(((bf16[4096,512]{1,0:T(8,128)(2,1)}), bf16[4096,512]{1,0:T(8,128)(2,1)}) %all-reduce.4.cloned.1.call-update) | async-done | bytes 4194320 | tf_op jit(solution)/shard_map/psum | solution.py:115
  1558.4 9.8 multiply_convert_fusion
  (65 shorter events, 52.3 us)
Async XLA Ops:
  7.2 64.0 %reduce-scatter.3.cloned.1.call-start = ((), (), s32[]{:S(2)}) async-start(), calls=%async_computation.2 | async-start | bytes 5242880 | tf_op jit(solution)/shard_map/reduce_scatter | solution.py:67
  15.1 1.0 copy-start.5
  15.1 1.3 copy-start.6
  15.1 131.4 %all-reduce.6.cloned.1.call-start = ((), (), s32[]{:S(2)}) async-start(), calls=%async_computation.7 | async-start | bytes 2228224 | tf_op jit(solution)/shard_map/psum | solution.py:81
  27.5 17.8 %collective-permute-start = (bf16[256,1088]{0,1:T(8,128)(2,1)S(1)}, bf16[256,1088]{0,1:T(8,128)(2,1)S(1)}, u32[]{:S(2)}, u32[]{:S(2)}) collective-permute-start(bf16[256,1088]{0,1:T(8,128)(2,1)S(1)} %get-tuple-element.16), channel_id=1, source_target_pairs={{0,8},{4,12},{8,16},{12,20},{16,24},{20,28},{24,0},{28,4},{1,9},{5... | collective-permute-start | bytes 1671176 | tf_op jit(solution)/shard_map/ppermute | solution.py:57
  29.3 35.9 %collective-permute-start.1 = (bf16[256,1088]{0,1:T(8,128)(2,1)S(1)}, bf16[256,1088]{0,1:T(8,128)(2,1)S(1)}, u32[]{:S(2)}, u32[]{:S(2)}) collective-permute-start(bf16[256,1088]{0,1:T(8,128)(2,1)S(1)} %get-tuple-element.17), channel_id=1, source_target_pairs={{0,16},{4,20},{8,24},{12,28},{16,0},{20,4},{24,8},{28,12},{1,17},{... | collective-permute-start | bytes 1671176 | tf_op jit(solution)/shard_map/ppermute | solution.py:57
  32.3 33.0 %collective-permute-start.2 = (bf16[256,1088]{0,1:T(8,128)(2,1)S(1)}, bf16[256,1088]{0,1:T(8,128)(2,1)S(1)}, u32[]{:S(2)}, u32[]{:S(2)}) collective-permute-start(bf16[256,1088]{0,1:T(8,128)(2,1)S(1)} %get-tuple-element.18), channel_id=1, source_target_pairs={{0,24},{4,28},{8,0},{12,4},{16,8},{20,12},{24,16},{28,20},{1,25},{... | collective-permute-start | bytes 1671176 | tf_op jit(solution)/shard_map/ppermute | solution.py:57
  65.2 0.8 copy-start.2
  65.2 1.0 copy-start.3
  77.6 97.6 %all-gather.6.cloned.1.call-start = ((), (), s32[]{:S(2)}) async-start(), calls=%async_computation.6 | async-start | bytes 1310720 | tf_op jit(solution)/shard_map/all_gather | solution.py:88
  81.9 68.1 %collective-permute-start.3 = (bf16[1024,1056]{0,1:T(8,128)(2,1)}, bf16[1024,1056]{0,1:T(8,128)(2,1)}, u32[]{:S(2)}, u32[]{:S(2)}) collective-permute-start(bf16[1024,1056]{0,1:T(8,128)(2,1)} %fusion.14), channel_id=1, source_target_pairs={{0,4},{4,0},{8,12},{12,8},{16,20},{20,16},{24,28},{28,24},{1,5},{5... | collective-permute-start | bytes 6488072 | tf_op jit(solution)/shard_map/ppermute | solution.py:64
  148.7 2.2 copy-start.4
  149.6 989.8 %reduce-scatter.5.cloned.1.call-start = ((), (), s32[]{:S(2)}) async-start(), calls=%async_computation.3 | async-start | bytes 5242880 | tf_op jit(solution)/shard_map/reduce_scatter | solution.py:113
  829.5 2.2 copy-start.1
  834.1 2.9 collective-permute-start.4
  839.5 47.8 %collective-permute-start.5 = (bf16[1024,1024]{0,1:T(8,128)(2,1)S(1)}, bf16[1024,1024]{0,1:T(8,128)(2,1)}, u32[]{:S(2)}, u32[]{:S(2)}) collective-permute-start(bf16[1024,1024]{0,1:T(8,128)(2,1)S(1)} %maximum_select_fusion.4), channel_id=1, source_target_pairs={{0,8},{4,12},{8,0},{12,4},{16,24},{20,28},{24,16},{28,20},{1,9},{5... | collective-permute-start | bytes 6291464 | tf_op jit(solution)/shard_map/ppermute | solution.py:15
  892.2 182.9 %collective-permute-start.6 = (bf16[1024,2048]{0,1:T(8,128)(2,1)}, bf16[1024,2048]{0,1:T(8,128)(2,1)}, u32[]{:S(2)}, u32[]{:S(2)}) collective-permute-start(bf16[1024,2048]{0,1:T(8,128)(2,1)} %maximum_select_fusion.2), channel_id=1, source_target_pairs={{0,16},{4,20},{8,24},{12,28},{16,0},{20,4},{24,8},{28,12},{1,17},{... | collective-permute-start | bytes 12582920 | tf_op jit(solution)/shard_map/ppermute | solution.py:15
  1086.7 107.8 %all-gather.4.cloned.1.call-start = ((), (), s32[]{:S(2)}) async-start(), calls=%async_computation.4 | async-start | bytes 5242880 | tf_op jit(solution)/shard_map/all_gather | solution.py:101
  1139.4 419.0 %all-reduce.4.cloned.1.call-start = ((), (), s32[]{:S(2)}) async-start(), calls=%async_computation.5 | async-start | bytes 8388608 | tf_op jit(solution)/shard_map/psum | solution.py:115
  1204.3 2.7 collective-permute-start.7
  1208.1 47.7 %collective-permute-start.8 = (bf16[1024,1024]{0,1:T(8,128)(2,1)S(1)}, bf16[1024,1024]{0,1:T(8,128)(2,1)S(1)}, u32[]{:S(2)}, u32[]{:S(2)}) collective-permute-start(bf16[1024,1024]{0,1:T(8,128)(2,1)S(1)} %maximum_select_fusion.5), channel_id=1, source_target_pairs={{0,8},{4,12},{8,0},{12,4},{16,24},{20,28},{24,16},{28,20},{1,9},{5... | collective-permute-start | bytes 6291464 | tf_op jit(solution)/shard_map/ppermute | solution.py:15
  1258.1 182.7 %copy-start = (bf16[1024,2048]{0,1:T(8,128)(2,1)}, bf16[1024,2048]{0,1:T(8,128)(2,1)S(1)}, u32[]{:S(2)}) copy-start(bf16[1024,2048]{0,1:T(8,128)(2,1)S(1)} %maximum_select_fusion.3) | copy-start | bytes 12582916
  1258.2 182.7 %collective-permute-start.9 = (bf16[1024,2048]{0,1:T(8,128)(2,1)S(1)}, bf16[1024,2048]{0,1:T(8,128)(2,1)}, u32[]{:S(2)}, u32[]{:S(2)}) collective-permute-start(bf16[1024,2048]{0,1:T(8,128)(2,1)S(1)} %maximum_select_fusion.3), channel_id=1, source_target_pairs={{0,16},{4,20},{8,24},{12,28},{16,0},{20,4},{24,8},{28,12},{1,17},{... | collective-permute-start | bytes 12582920 | tf_op jit(solution)/shard_map/ppermute | solution.py:15
Sparse Core Ops, SparseCore 0:
  15.2 55.9 reduce-scatter.2
  77.7 68.7 all-reduce.5
  149.7 25.4 all-gather.5
  1086.8 52.5 reduce-scatter.4
  1141.1 53.3 all-gather.3
  1454.8 103.5 all-reduce.3
